TPU v7x, 256 devices: a whole 4x4x8 slice. The times are simulated.
256 devices in a mesh: seq: 16 (over z, y_lo), chan: 16 (over y_hi, x, core).
Axes of the slice: x: 4, y: 4 (y_hi: 2, y_lo: 2; y = y_hi * 2 + y_lo), z: 8, core: 2. Of those that a mesh axis runs over, the one named last changes fastest.
Arguments:
- tokens: bfloat16 [4096, 4096], P('seq', 'chan'), may hold values from -6 to 6
- in_weight: bfloat16 [4096, 3, 4096], P(None, None, 'chan'), may hold values from -0.09375 to 0.09375
- short_weight: float32 [3, 3, 4096], P(None, None, 'chan'), may hold values from -3 to 3
- filter_taps: bfloat16 [4096, 4096], P(None, 'chan'), may hold values from -0.09375 to 0.09375
- cotangent: bfloat16 [4096, 4096], P('seq', 'chan'), may hold values from -1.5 to 1.5
Outputs:
- operator_out: bfloat16 [4096, 4096], P('seq', 'chan')
- stream_grads: bfloat16 [4096, 3, 4096], P('seq', None, 'chan')
- tap_grads: float32 [4096, 4096], P('seq', 'chan')
All inputs are finite; a program needn't handle non-finite values.
Results may differ from a plain program's by a relative error of at most 0.015.
Values may be sent and summed in bfloat16 or wider, within the bound.
No kernel may reach another device: no remote copies, remote signals or barrier semaphores. Data moves between devices by JAX's collectives and lax.ppermute only.
A program may use at most 128 MiB of HBM per device.

v0:
```python
import math
import jax
import jax.numpy as jnp
from jax import lax
from jax.sharding import PartitionSpec as P


def passed_along(block, axis, distance):
    devices = range(lax.axis_size(axis))
    route = [(i - distance, i) for i in devices if i - distance in devices]
    return lax.ppermute(block, axis, route)


def dft_tables(row_count):
    length = 2 * row_count
    sample = jnp.arange(length, dtype=jnp.int32)
    frequency = jnp.arange(row_count, dtype=jnp.int32)
    angles = (frequency[:, None] * sample[None, :] % length).astype(jnp.float32) * (
        2.0 * math.pi / length
    )
    parity = 1.0 - 2.0 * (sample % 2).astype(jnp.float32)
    lower_rows = jnp.where(frequency[:, None] == 0, parity[None, :], -jnp.sin(angles))
    forward = jnp.concatenate([jnp.cos(angles), lower_rows], axis=0)
    out_index = row_count + frequency
    back_angles = (out_index[:, None] * frequency[None, :] % length).astype(jnp.float32) * (
        2.0 * math.pi / length
    )
    factor = jnp.where(frequency == 0, 1.0, 2.0) / length
    out_parity = 1.0 - 2.0 * (out_index % 2).astype(jnp.float32)
    real_part = jnp.cos(back_angles) * factor[None, :]
    imag_part = jnp.where(
        frequency[None, :] == 0, out_parity[:, None] / length, -2.0 * jnp.sin(back_angles) / length
    )
    inverse = jnp.concatenate([real_part, imag_part], axis=1)
    return (forward, inverse)


def spectral_product(left_spec, right_spec):
    half_len = left_spec.shape[0] // 2
    left_spec = left_spec.astype(jnp.float32)
    right_spec = right_spec.astype(jnp.float32)
    left_re, left_im = (left_spec[:half_len], left_spec[half_len:])
    right_re, right_im = (right_spec[:half_len], right_spec[half_len:])
    first_row = (jnp.arange(half_len) == 0).reshape((half_len,) + (1,) * (left_spec.ndim - 1))
    cross_term = left_im * right_im
    real_out = left_re * right_re - jnp.where(first_row, 0.0, cross_term)
    imag_out = jnp.where(first_row, cross_term, left_re * right_im + left_im * right_re)
    return jnp.concatenate([real_out, imag_out], axis=0)


def spectral_adjoint(left_spec, grad_spec):
    half_len = left_spec.shape[0] // 2
    left_spec = left_spec.astype(jnp.float32)
    grad_spec = grad_spec.astype(jnp.float32)
    left_re, left_im = (left_spec[:half_len], left_spec[half_len:])
    grad_re, grad_im = (grad_spec[:half_len], grad_spec[half_len:])
    first_row = (jnp.arange(half_len) == 0).reshape((half_len,) + (1,) * (left_spec.ndim - 1))
    cross_term = left_im * grad_im
    real_out = left_re * grad_re + jnp.where(first_row, 0.0, cross_term)
    imag_out = jnp.where(first_row, cross_term, left_re * grad_im - left_im * grad_re)
    return jnp.concatenate([real_out, imag_out], axis=0)


def neighbour_rows(edge_rows, offset):
    return passed_along(edge_rows, "seq", offset)


def on_device(tokens, in_weight, short_weight, filter_taps, cotangent):
    row_count, local_width = tokens.shape
    spec_rows = 2 * row_count
    seq_count = lax.axis_size("seq")
    own_block = lax.axis_index("seq")
    forward, inverse = dft_tables(row_count)
    full_table = forward.astype(jnp.bfloat16)
    half_table = full_table[:, :row_count]
    back_table = inverse.astype(jnp.bfloat16)
    weight_cols = in_weight.reshape(in_weight.shape[0], 3 * local_width)
    streams = jnp.dot(
        lax.all_gather(tokens, "chan", axis=1, tiled=True),
        weight_cols,
        preferred_element_type=jnp.float32,
    )
    streams = streams.astype(jnp.bfloat16)
    before = neighbour_rows(streams[row_count - 2 :], 1)
    extended = (
        jnp.concatenate([before, streams], axis=0)
        .astype(jnp.float32)
        .reshape(row_count + 2, 3, local_width)
    )
    conv_out = (
        short_weight[:, 0] * extended[2:]
        + short_weight[:, 1] * extended[1:-1]
        + short_weight[:, 2] * extended[:-2]
    )
    query_conv, key_conv, value_conv = (conv_out[:, 0], conv_out[:, 1], conv_out[:, 2])
    gated = (key_conv * value_conv).astype(jnp.bfloat16)
    own_spec = jnp.dot(half_table, gated, preferred_element_type=jnp.float32).astype(jnp.bfloat16)
    tap_blocks = filter_taps.reshape(seq_count, row_count, local_width)
    earlier = jnp.concatenate(
        [jnp.zeros((1, row_count, local_width), jnp.bfloat16), tap_blocks[:-1]], axis=0
    )
    segments = jnp.concatenate([earlier, tap_blocks], axis=1)
    filters = jnp.einsum(
        "fn,bnc->bfc", full_table, segments, preferred_element_type=jnp.float32
    ).astype(jnp.bfloat16)
    pieces = lax.all_gather(own_spec, "seq", axis=0, tiled=True)

    def forward_add_block(position, carried):
        lag_index = own_block - position
        incoming = lax.dynamic_slice_in_dim(pieces, position * spec_rows, spec_rows, 0)
        filter_spec = lax.dynamic_index_in_dim(
            filters, jnp.clip(lag_index, 0, seq_count - 1), 0, keepdims=False
        )
        return carried + jnp.where(lag_index >= 0, spectral_product(filter_spec, incoming), 0.0)

    mixed_spec = lax.fori_loop(
        0,
        pieces.shape[0] // spec_rows,
        forward_add_block,
        jnp.zeros((spec_rows, local_width), jnp.float32),
    )
    long_out = jnp.dot(
        back_table, mixed_spec.astype(jnp.bfloat16), preferred_element_type=jnp.float32
    ).astype(jnp.bfloat16)
    operator_out = (query_conv * long_out.astype(jnp.float32)).astype(jnp.bfloat16)
    cot_wide = cotangent.astype(jnp.float32)
    grad_long = (cot_wide * query_conv).astype(jnp.bfloat16)
    grad_query = cot_wide * long_out.astype(jnp.float32)
    grad_spec = jnp.dot(back_table.T, grad_long, preferred_element_type=jnp.float32).astype(
        jnp.bfloat16
    )
    start_state = (
        jnp.zeros((spec_rows, local_width), jnp.float32),
        jnp.zeros((seq_count, spec_rows, local_width), jnp.float32),
    )
    backward_pieces = lax.all_gather(grad_spec, "seq", axis=0, tiled=True)

    def backward_add_block(position, state):
        spectral_grad, filter_grad = state
        lag_index = position - own_block
        usable = lag_index >= 0
        clipped = jnp.clip(lag_index, 0, seq_count - 1)
        incoming = lax.dynamic_slice_in_dim(backward_pieces, position * spec_rows, spec_rows, 0)
        filter_spec = lax.dynamic_index_in_dim(filters, clipped, 0, keepdims=False)
        spectral_grad = spectral_grad + jnp.where(
            usable, spectral_adjoint(filter_spec, incoming), 0.0
        )
        current = lax.dynamic_index_in_dim(filter_grad, clipped, 0, keepdims=False)
        current = current + jnp.where(usable, spectral_adjoint(own_spec, incoming), 0.0)
        filter_grad = lax.dynamic_update_index_in_dim(filter_grad, current, clipped, 0)
        return (spectral_grad, filter_grad)

    spectral_grad, filter_grad = lax.fori_loop(
        0, backward_pieces.shape[0] // spec_rows, backward_add_block, start_state
    )
    grad_gated = jnp.dot(
        half_table.T, spectral_grad.astype(jnp.bfloat16), preferred_element_type=jnp.float32
    ).astype(jnp.bfloat16)
    tap_spec = jnp.einsum("fn,bfc->bnc", forward, filter_grad, precision=lax.Precision.HIGHEST)
    tap_terms = tap_spec[:, row_count:] + jnp.concatenate(
        [tap_spec[1:, :row_count], jnp.zeros((1, row_count, local_width), jnp.float32)], axis=0
    )
    tap_grads = lax.psum_scatter(
        tap_terms.reshape(seq_count * row_count, local_width).astype(jnp.bfloat16),
        "seq",
        scatter_dimension=0,
        tiled=True,
    ).astype(jnp.float32)
    gated_wide = grad_gated.astype(jnp.float32)
    grad_streams = jnp.stack(
        [grad_query, gated_wide * value_conv, gated_wide * key_conv], axis=1
    ).astype(jnp.bfloat16)
    grad_streams = grad_streams.reshape(row_count, 3 * local_width)
    after = neighbour_rows(grad_streams[:2], -1)
    padded = (
        jnp.concatenate([grad_streams, after], axis=0)
        .astype(jnp.float32)
        .reshape(row_count + 2, 3, local_width)
    )
    stream_grads = (
        short_weight[:, 0] * padded[:row_count]
        + short_weight[:, 1] * padded[1 : row_count + 1]
        + short_weight[:, 2] * padded[2:]
    ).astype(jnp.bfloat16)
    return (operator_out, stream_grads, tap_grads)


def solution(mesh):
    return jax.shard_map(
        on_device,
        mesh=mesh,
        in_specs=(
            P("seq", "chan"),
            P(None, None, "chan"),
            P(None, None, "chan"),
            P(None, "chan"),
            P("seq", "chan"),
        ),
        out_specs=(P("seq", "chan"), P("seq", None, "chan"), P("seq", "chan")),
        check_vma=False,
    )
```

profile of v0, /device:TPU:20, one launch (start us, length us, event | category | flops | bytes accessed | tf_op | source)
XLA Modules:
  0.0 376.9 jit_solution(4375459504469983553)
XLA Ops:
  8.0 8.7 %copy.31 = bf16[4096,3,256]{0,2,1:T(8,128)(2,1)} copy(bf16[4096,3,256]{2,0,1:T(8,128)(2,1)} %param.10) | data formatting | bytes 12582912 | tf_op args[1]
  16.7 1.1 multiply_convert_fusion.2
  17.8 1.1 select_convert_fusion
  18.9 44.9 %all-gather.4.cloned.1.call-done = bf16[256,4096]{1,0:T(8,128)(2,1)} async-done(((bf16[256,256]{1,0:T(8,128)(2,1)}), bf16[256,4096]{1,0:T(8,128)(2,1)}) %all-gather.4.cloned.1.call-update) | async-done | bytes 2097168 | tf_op jit(solution)/shard_map/all_gather | solution.py:79
  63.8 5.2 %convolution_convert_fusion = bf16[256,768]{1,0:T(8,128)(2,1)S(1)} fusion(bf16[256,4096]{1,0:T(8,128)(2,1)} %all-gather.4.cloned.1.call-done, bf16[4096,768]{0,1:T(8,128)(2,1)} %bitcast.104), kind=kOutput, calls=%fused_computation.38 | convolution fusion | flops 1610809344 | bytes 8781824 | tf_op jit(solution)/shard_map/dot_general | solution.py:78
  69.0 4.0 %collective-permute-start = (bf16[2,768]{1,0:T(2,128)(2,1)S(1)}, bf16[2,768]{1,0:T(2,128)(2,1)S(1)}, u32[]{:S(2)}, u32[]{:S(2)}) collective-permute-start(bf16[2,768]{1,0:T(2,128)(2,1)S(1)} %slice.215), channel_id=1, source_target_pairs={{0,16},{16,32},{32,48},{48,64},{64,80},{80,96},{96,112},{112,128},... | collective-permute-start | bytes 9224 | tf_op jit(solution)/shard_map/ppermute | solution.py:11
  73.1 1.3 collective-permute-done
  74.9 1.2 copy.33
  76.3 1.2 copy.37
  77.8 1.2 copy.35
  79.0 1.9 multiply_add_fusion
  82.0 2.3 copy.38
  84.3 3.9 %copy.39 = bf16[16,256,256]{1,2,0:T(8,128)(2,1)} copy(bf16[16,256,256]{2,1,0:T(8,128)(2,1)} %bitcast.102) | data formatting | bytes 4194304 | tf_op jit(solution)/shard_map/reshape | solution.py:98
  88.2 2.1 negate_select_fusion.2
  90.4 6.7 %convert_bitcast_fusion = bf16[16,512,256]{1,2,0:T(8,128)(2,1)} fusion(bf16[15,256,256]{1,2,0:T(8,128)(2,1)} %copy.38, bf16[16,256,256]{1,2,0:T(8,128)(2,1)} %copy.39, bf16[512,512]{1,0:T(8,128)(2,1)S(1)} %fusion.20), kind=kOutput, calls=%fused_computation.35 | convolution fusion | flops 2162163712 | bytes 8781824 | tf_op jit(solution)/shard_map/fn,bnc->bfc/dot_general | solution.py:103
  97.1 6.4 %copy.40 = bf16[16,512,256]{2,1,0:T(8,128)(2,1)} copy(bf16[16,512,256]{1,2,0:T(8,128)(2,1)} %convert_bitcast_fusion) | data formatting | bytes 8388608
  103.5 2.0 convolution_convert_fusion.2
  105.7 79.7 %all-gather.8.cloned.1.call-done = bf16[8192,256]{1,0:T(8,128)(2,1)} async-done(((bf16[512,256]{1,0:T(8,128)(2,1)}), bf16[8192,256]{1,0:T(8,128)(2,1)}) %all-gather.8.cloned.1.call-update) | async-done | bytes 4194320 | tf_op jit(solution)/shard_map/all_gather | solution.py:136
  185.4 4.2 %broadcast_in_dim.154 = f32[16,512,256]{2,1,0:T(8,128)} broadcast(f32[]{:T(128)} %constant.182.clone.1), dimensions={} | broadcast | bytes 8388612 | tf_op jit(solution)/shard_map/broadcast_in_dim | solution.py:134
  189.6 69.7 %while.31 = (s32[]{:T(128)}, f32[512,256]{1,0:T(8,128)S(1)}, f32[16,512,256]{2,1,0:T(8,128)}, s32[]{:T(128)}, bf16[16,512,256]{2,1,0:T(8,128)(2,1)}, /*index=5*/...) while((s32[]{:T(128)}, f32[512,256]{1,0:T(8,128)S(1)}, ...), condition=%wide.region_3.4_spmd.clone, body=%wide.region_2.3_spmd.clone.sunk | while | flops 2359563 | bytes 8127216 | solution.py:153
  192.0 1.9 fusion.74
  196.4 1.9 fusion.74
  200.7 1.9 fusion.74
  205.1 1.9 fusion.74
  209.4 1.9 fusion.74
  213.8 1.9 fusion.74
  218.1 1.9 fusion.74
  221.1 1.0 dynamic-slice_convert_fusion.11
  222.5 1.9 fusion.74
  226.8 1.9 fusion.74
  231.2 1.9 fusion.74
  235.6 1.9 fusion.74
  238.5 1.0 dynamic-slice_convert_fusion.11
  239.9 1.9 fusion.74
  242.9 1.0 dynamic-slice_convert_fusion.11
  244.3 1.9 fusion.74
  248.6 1.9 fusion.74
  251.6 1.0 dynamic-slice_convert_fusion.11
  253.0 1.9 fusion.74
  255.9 1.0 dynamic-slice_convert_fusion.11
  257.3 2.0 fusion.74
  259.3 16.5 %convolution_bitcast_fusion = f32[16,512,256]{1,2,0:T(8,128)S(1)} fusion(f32[16,512,256]{2,1,0:T(8,128)} %get-tuple-element.224, f32[256,512]{1,0:T(8,128)S(1)} %get-tuple-element.350, f32[256,512]{1,0:T(8,128)S(1)} %get-tuple-element.351), kind=kOutput, calls=%fused_computation.36 | convolution fusion | flops 12885164032 | bytes 17825792 | tf_op jit(solution)/shard_map/fn,bfc->bnc/dot_general | solution.py:159
  277.3 2.4 copy.48
  279.8 6.8 %all-gather.6.cloned.1.call-done = bf16[8192,256]{1,0:T(8,128)(2,1)} async-done(((bf16[512,256]{1,0:T(8,128)(2,1)}), bf16[8192,256]{1,0:T(8,128)(2,1)}) %all-gather.6.cloned.1.call-update) | async-done | bytes 4194320 | tf_op jit(solution)/shard_map/all_gather | solution.py:106
  286.6 37.5 %while.30 = (s32[]{:T(128)}, f32[512,256]{1,0:T(8,128)S(1)}, s32[]{:T(128)}, bf16[16,512,256]{2,1,0:T(8,128)(2,1)}, bf16[8192,256]{1,0:T(8,128)(2,1)}, /*index=5...) while((s32[]{:T(128)}, f32[512,256]{1,0:T(8,128)S(1)}, s32[]{:T(128)}, ...), condition=%wide.region_1.2_spmd.clone, body=%wide.region_0.1_spmd.clone.sunk | while | flops 1310987 | bytes 4719323 | solution.py:116
  286.6 1.1 dynamic-slice_convert_fusion.9
  291.4 1.0 dynamic-slice_convert_fusion.9
  293.7 1.0 dynamic-slice_convert_fusion.9
  296.0 1.0 dynamic-slice_convert_fusion.9
  298.4 1.0 dynamic-slice_convert_fusion.9
  300.7 1.0 dynamic-slice_convert_fusion.9
  306.4 1.0 dynamic-slice_convert_fusion.8
  308.7 1.0 dynamic-slice_convert_fusion.8
  310.0 1.0 dynamic-slice_convert_fusion.9
  311.0 1.0 dynamic-slice_convert_fusion.8
  314.7 1.0 dynamic-slice_convert_fusion.9
  315.7 1.0 dynamic-slice_convert_fusion.8
  318.0 1.0 dynamic-slice_convert_fusion.8
  319.4 1.0 dynamic-slice_convert_fusion.9
  322.7 1.0 dynamic-slice_convert_fusion.8
  325.5 1.3 collective-permute-start.1
  327.0 10.7 %collective-permute-done.1 = bf16[2,768]{0,1:T(8,128)(2,1)S(1)} collective-permute-done((bf16[2,768]{0,1:T(8,128)(2,1)S(1)}, bf16[2,768]{0,1:T(8,128)(2,1)S(1)}, u32[]{:S(2)}, u32[]{:S(2)}) %collective-permute-start.1) | collective-permute-done | bytes 3104 | tf_op jit(solution)/shard_map/ppermute | solution.py:11
  340.0 28.7 %reduce-scatter.2.cloned.1.call-done = bf16[256,256]{1,0:T(8,128)(2,1)} async-done(((bf16[4096,256]{1,0:T(8,128)(2,1)}), bf16[256,256]{1,0:T(8,128)(2,1)}) %reduce-scatter.2.cloned.1.call-update) | async-done | bytes 131088 | tf_op jit(solution)/shard_map/reduce_scatter | solution.py:163
  368.8 1.6 convert_element_type.164
  (217 shorter events, 63.7 us)
Async XLA Ops:
  7.2 56.6 %all-gather.4.cloned.1.call-start = ((), (), s32[]{:S(2)}) async-start(), calls=%async_computation.1 | async-start | bytes 2228224 | tf_op jit(solution)/shard_map/all_gather | solution.py:79
  7.9 8.8 %copy-start.8 = (f32[3,3,256]{2,1,0:T(4,128)S(1)}, f32[3,3,256]{2,1,0:T(4,128)}, u32[]{:S(2)}) copy-start(f32[3,3,256]{2,1,0:T(4,128)} %param.11) | copy-start | bytes 27652
  7.9 177.5 %all-gather.8.cloned.1.call-start = ((), (), s32[]{:S(2)}) async-start(), calls=%async_computation.3 | async-start | bytes 4456448 | tf_op jit(solution)/shard_map/all_gather | solution.py:136
  18.9 62.0 %copy-start.5 = (bf16[256,256]{1,0:T(8,128)(2,1)}, bf16[256,256]{1,0:T(8,128)(2,1)S(1)}, u32[]{:S(2)}) copy-start(bf16[256,256]{1,0:T(8,128)(2,1)S(1)} %select_convert_fusion) | copy-start | bytes 393220
  69.0 5.3 %collective-permute-start = (bf16[2,768]{1,0:T(2,128)(2,1)S(1)}, bf16[2,768]{1,0:T(2,128)(2,1)S(1)}, u32[]{:S(2)}, u32[]{:S(2)}) collective-permute-start(bf16[2,768]{1,0:T(2,128)(2,1)S(1)} %slice.215), channel_id=1, source_target_pairs={{0,16},{16,32},{32,48},{48,64},{64,80},{80,96},{96,112},{112,128},... | collective-permute-start | bytes 9224 | tf_op jit(solution)/shard_map/ppermute | solution.py:11
  76.3 4.6 %copy-start.7 = (bf16[256,256]{1,0:T(8,128)(2,1)S(1)}, bf16[256,256]{1,0:T(8,128)(2,1)}, u32[]{:S(2)}) copy-start(bf16[256,256]{1,0:T(8,128)(2,1)} %param.13) | copy-start | bytes 393220
  79.0 3.0 slice-start
  80.9 1.1 copy-start.1
  81.9 204.6 %all-gather.6.cloned.1.call-start = ((), (), s32[]{:S(2)}) async-start(), calls=%async_computation.2 | async-start | bytes 4456448 | tf_op jit(solution)/shard_map/all_gather | solution.py:106
  90.4 13.1 %copy-start.3 = (bf16[512,512]{1,0:T(8,128)(2,1)}, bf16[512,512]{1,0:T(8,128)(2,1)S(1)}, u32[]{:S(2)}) copy-start(bf16[512,512]{1,0:T(8,128)(2,1)S(1)} %fusion.20) | copy-start | bytes 1572868
  105.5 84.1 %copy-start = (bf16[512,256]{1,0:T(8,128)(2,1)S(1)}, bf16[512,256]{1,0:T(8,128)(2,1)}, u32[]{:S(2)}) copy-start(bf16[512,256]{1,0:T(8,128)(2,1)} %convolution_convert_fusion.2) | copy-start | bytes 786436
  105.5 263.3 %reduce-scatter.2.cloned.1.call-start = ((), (), s32[]{:S(2)}) async-start(), calls=%async_computation.4 | async-start | bytes 2228224 | tf_op jit(solution)/shard_map/reduce_scatter | solution.py:163
  286.6 37.5 %copy-start.2 = (f32[256,3,256]{2,0,1:T(8,128)S(1)}, f32[256,3,256]{2,0,1:T(8,128)}, u32[]{:S(2)}) copy-start(f32[256,3,256]{2,0,1:T(8,128)} %copy-done.1) | copy-start | bytes 2359300
  286.6 37.5 %copy-start.4 = (bf16[512,512]{1,0:T(8,128)(2,1)S(1)}, bf16[512,512]{1,0:T(8,128)(2,1)}, u32[]{:S(2)}) copy-start(bf16[512,512]{1,0:T(8,128)(2,1)} %copy-done.3) | copy-start | bytes 1572868
  286.6 37.8 %copy-start.6 = (bf16[256,256]{1,0:T(8,128)(2,1)S(1)}, bf16[256,256]{1,0:T(8,128)(2,1)}, u32[]{:S(2)}) copy-start(bf16[256,256]{1,0:T(8,128)(2,1)} %copy-done.5) | copy-start | bytes 393220
  325.5 12.2 %collective-permute-start.1 = (bf16[2,768]{0,1:T(8,128)(2,1)S(1)}, bf16[2,768]{0,1:T(8,128)(2,1)S(1)}, u32[]{:S(2)}, u32[]{:S(2)}) collective-permute-start(bf16[2,768]{0,1:T(8,128)(2,1)S(1)} %copy.43), channel_id=1, source_target_pairs={{16,0},{32,16},{48,32},{64,48},{80,64},{96,80},{112,96},{128,112},... | collective-permute-start | bytes 9224 | tf_op jit(solution)/shard_map/ppermute | solution.py:11
Sparse Core Ops, SparseCore 0:
  10.5 53.1 all-gather.3
  82.0 103.3 all-gather.7
  187.8 98.7 all-gather.5
  288.9 79.7 reduce-scatter.1
where the time goes:
time: 380 us; the launch traced here: 377 us
  waiting for transfers between devices  173 us (46%)
  other arithmetic  116 us (31%)
  local copies, waits for them, and re-layouts  34.6 us (9%)
  matrix products  32.6 us (9%)
  between operations  14.1 us (4%)
  starting transfers between devices  5.63 us (1%)
    all_gather x1, waiting for transfers between devices, on_device(): backward_pieces = lax.all_gather(grad_spec, 'seq', axis=0, tiled=True)  79.7 us
    all_gather x1, waiting for transfers between devices, on_device(): lax.all_gather(tokens, 'chan', axis=1, tiled=True)  44.9 us
    dynamic_update_slice x16, other arithmetic, backward_add_block(): lax.dynamic_update_index_in_dim(filter_grad, current, clipped, 0)  30.7 us
    reduce_scatter x1, waiting for transfers between devices, on_device(): lax.psum_scatter(tap_terms.reshape(seq_count * row_count, local_width).as...  28.7 us
    dot_general x1, matrix products, on_device(): jnp.einsum('fn,bfc->bnc', forward, filter_grad, precision=lax.Precision.H...  16.5 us
    convert_element_type x32, other arithmetic, spectral_adjoint(): left_spec = left_spec.astype(jnp.float32)  16.5 us
    convert_element_type x16, other arithmetic, spectral_product(): right_spec = right_spec.astype(jnp.float32)  16 us
    convert_element_type x16, other arithmetic, spectral_product(): left_spec = left_spec.astype(jnp.float32)  15.9 us
  transfers between devices with their start and end apart: 6, of which 6 were waited for; matrix products, arithmetic and copies ran while one was open for 45% of the time, Pallas kernels for 0%

commit v1 on v0

--- a/solution.py
+++ b/solution.py
@@ -133,7 +133,10 @@
         jnp.zeros((spec_rows, local_width), jnp.float32),
         jnp.zeros((seq_count, spec_rows, local_width), jnp.float32),
     )
-    backward_pieces = lax.all_gather(grad_spec, "seq", axis=0, tiled=True)
+    sides = []
+    for _ in range(lax.psum(1, "seq")):
+        sides.append(grad_spec)
+    backward_pieces = jnp.concatenate(lax.all_to_all(jnp.stack(sides, axis=0), "seq", 0, 0), axis=0)
 
     def backward_add_block(position, state):
         spectral_grad, filter_grad = state

time: 380 us -> 400 us (1.053)
  waiting for transfers between devices: 173 us -> 184 us
  starting transfers between devices: 5.63 us -> 15.4 us
    all_gather x1 -> x0, waiting for transfers between devices: 79.7 us -> none  [on_device(): backward_pieces = lax.all_gather(grad_spec, 'seq', axis=0, tiled=True)]
    all_to_all x0 -> x1, waiting for transfers between devices: none -> 76.4 us  [on_device(): lax.all_to_all(jnp.stack(sides, axis=0), 'seq', 0, 0)]
    reduce_scatter x1, waiting for transfers between devices: 28.7 us -> 40.5 us  [on_device(): lax.psum_scatter(tap_terms.reshape(seq_count * row_count, local_width).as...]
    ppermute x2, waiting for transfers between devices: 12 us -> 21.6 us  [passed_along(): return lax.ppermute(block, axis, route)]
    all_to_all x0 -> x1, starting transfers between devices: none -> 9.6 us  [on_device(): lax.all_to_all(jnp.stack(sides, axis=0), 'seq', 0, 0)]
    all_gather x1, waiting for transfers between devices: 6.8 us -> 0.02 us  [on_device(): pieces = lax.all_gather(own_spec, 'seq', axis=0, tiled=True)]
  transfers between devices with their start and end apart: 6 -> 6, of which waited for: 6 -> 5; matrix products, arithmetic and copies ran while one was open for 45% -> 43% of each run, Pallas kernels for 0% -> 0%
where the time goes in v1:
time: 400 us; the launch traced here: 396 us
  waiting for transfers between devices  184 us (46%)
  other arithmetic  114 us (28%)
  local copies, waits for them, and re-layouts  34.2 us (9%)
  matrix products  33 us (8%)
  starting transfers between devices  15.4 us (4%)
  between operations  14.2 us (4%)
    all_to_all x1, waiting for transfers between devices, on_device(): lax.all_to_all(jnp.stack(sides, axis=0), 'seq', 0, 0)  76.4 us
    all_gather x1, waiting for transfers between devices, on_device(): lax.all_gather(tokens, 'chan', axis=1, tiled=True)  44.9 us
    reduce_scatter x1, waiting for transfers between devices, on_device(): lax.psum_scatter(tap_terms.reshape(seq_count * row_count, local_width).as...  40.5 us
    dynamic_update_slice x16, other arithmetic, backward_add_block(): lax.dynamic_update_index_in_dim(filter_grad, current, clipped, 0)  30.8 us
    ppermute x2, waiting for transfers between devices, passed_along(): return lax.ppermute(block, axis, route)  21.6 us
    dot_general x1, matrix products, on_device(): jnp.einsum('fn,bfc->bnc', forward, filter_grad, precision=lax.Precision.H...  16.5 us
    convert_element_type x32, other arithmetic, spectral_adjoint(): left_spec = left_spec.astype(jnp.float32)  16.5 us
    convert_element_type x16, other arithmetic, spectral_product(): right_spec = right_spec.astype(jnp.float32)  16 us
  transfers between devices with their start and end apart: 6, of which 5 were waited for; matrix products, arithmetic and copies ran while one was open for 43% of the time, Pallas kernels for 0%

profile of v1, /device:TPU:20, one launch (start us, length us, event | category | flops | bytes accessed | tf_op | source)
XLA Modules:
  0.0 396.5 jit_solution(13066291833006537460)
XLA Ops:
  7.9 8.7 %copy.31 = bf16[4096,3,256]{0,2,1:T(8,128)(2,1)} copy(bf16[4096,3,256]{2,0,1:T(8,128)(2,1)} %param.10) | data formatting | bytes 12582912 | tf_op args[1]
  16.7 1.1 multiply_convert_fusion.2
  17.8 1.1 select_convert_fusion
  18.9 44.9 %all-gather.3.cloned.1.call-done = bf16[256,4096]{1,0:T(8,128)(2,1)} async-done(((bf16[256,256]{1,0:T(8,128)(2,1)}), bf16[256,4096]{1,0:T(8,128)(2,1)}) %all-gather.3.cloned.1.call-update) | async-done | bytes 2097168 | tf_op jit(solution)/shard_map/all_gather | solution.py:79
  63.8 5.2 %convolution_convert_fusion = bf16[256,768]{1,0:T(8,128)(2,1)S(1)} fusion(bf16[256,4096]{1,0:T(8,128)(2,1)} %all-gather.3.cloned.1.call-done, bf16[4096,768]{0,1:T(8,128)(2,1)} %bitcast.105), kind=kOutput, calls=%fused_computation.38 | convolution fusion | flops 1610809344 | bytes 8781824 | tf_op jit(solution)/shard_map/dot_general | solution.py:78
  69.0 4.0 %collective-permute-start = (bf16[2,768]{1,0:T(2,128)(2,1)S(1)}, bf16[2,768]{1,0:T(2,128)(2,1)S(1)}, u32[]{:S(2)}, u32[]{:S(2)}) collective-permute-start(bf16[2,768]{1,0:T(2,128)(2,1)S(1)} %slice.215), channel_id=1, source_target_pairs={{0,16},{16,32},{32,48},{48,64},{64,80},{80,96},{96,112},{112,128},... | collective-permute-start | bytes 9224 | tf_op jit(solution)/shard_map/ppermute | solution.py:11
  73.1 1.3 collective-permute-done
  76.4 1.3 convolution_convert_fusion.1
  77.7 2.4 stack.11
  80.1 9.6 %all-to-all-start = ((bf16[16,512,256]{2,1,0:T(8,128)(2,1)}), bf16[16,512,256]{2,1,0:T(8,128)(2,1)}, u32[]{:S(2)}, u32[]{:S(2)}) async-start(bf16[16,512,256]{2,1,0:T(8,128)(2,1)} %stack.11), calls=%async_computation | async-start | bytes 8388608 | tf_op jit(solution)/shard_map/all_to_all | solution.py:139
  90.0 2.3 copy.38
  92.3 3.9 copy.39
  96.2 2.1 negate_select_fusion.2
  98.5 6.8 %convert_bitcast_fusion = bf16[16,512,256]{1,2,0:T(8,128)(2,1)} fusion(bf16[15,256,256]{1,2,0:T(8,128)(2,1)} %copy.38, bf16[16,256,256]{1,2,0:T(8,128)(2,1)} %copy.39, bf16[512,512]{1,0:T(8,128)(2,1)S(1)} %fusion.20), kind=kOutput, calls=%fused_computation.35 | convolution fusion | flops 2162163712 | bytes 8781824 | tf_op jit(solution)/shard_map/fn,bnc->bfc/dot_general | solution.py:103
  105.2 6.4 %copy.40 = bf16[16,512,256]{2,1,0:T(8,128)(2,1)} copy(bf16[16,512,256]{1,2,0:T(8,128)(2,1)} %convert_bitcast_fusion) | data formatting | bytes 8388608
  111.6 2.0 convolution_convert_fusion.2
  113.9 76.4 %all-to-all-done = bf16[16,512,256]{2,1,0:T(8,128)(2,1)} async-done(((bf16[16,512,256]{2,1,0:T(8,128)(2,1)}), bf16[16,512,256]{2,1,0:T(8,128)(2,1)}, u32[]{:S(2)}, u32[]{:S(2)}) %all-to-all-start) | async-done | bytes 4194336 | tf_op jit(solution)/shard_map/all_to_all | solution.py:139
  190.2 4.1 %broadcast_in_dim.154 = f32[16,512,256]{2,1,0:T(8,128)} broadcast(f32[]{:T(128)} %constant.182.clone.1), dimensions={} | broadcast | bytes 8388612 | tf_op jit(solution)/shard_map/broadcast_in_dim | solution.py:134
  194.4 69.8 %while.31 = (s32[]{:T(128)}, f32[512,256]{1,0:T(8,128)S(1)}, f32[16,512,256]{2,1,0:T(8,128)}, s32[]{:T(128)}, bf16[16,512,256]{2,1,0:T(8,128)(2,1)}, /*index=5*/...) while((s32[]{:T(128)}, f32[512,256]{1,0:T(8,128)S(1)}, ...), condition=%wide.region_3.4_spmd.clone, body=%wide.region_2.3_spmd.clone.sunk | while | flops 2359563 | bytes 8127216 | solution.py:156
  196.8 1.9 fusion.74
  199.8 1.0 dynamic-slice_convert_fusion.11
  201.2 1.9 fusion.74
  205.5 1.9 fusion.74
  209.9 1.9 fusion.74
  214.2 1.9 fusion.74
  218.6 1.9 fusion.74
  223.0 1.9 fusion.74
  227.3 1.9 fusion.74
  230.3 1.0 dynamic-slice_convert_fusion.11
  231.7 1.9 fusion.74
  234.6 1.0 dynamic-slice_convert_fusion.11
  236.0 1.9 fusion.74
  240.4 1.9 fusion.74
  243.4 1.0 dynamic-slice_convert_fusion.11
  244.8 1.9 fusion.74
  247.7 1.0 dynamic-slice_convert_fusion.11
  249.1 1.9 fusion.74
  253.5 1.9 fusion.74
  257.8 1.9 fusion.74
  262.2 2.0 fusion.74
  264.2 16.5 %convolution_bitcast_fusion = f32[16,512,256]{1,2,0:T(8,128)S(1)} fusion(f32[16,512,256]{2,1,0:T(8,128)} %get-tuple-element.224, f32[256,512]{1,0:T(8,128)S(1)} %get-tuple-element.350, f32[256,512]{1,0:T(8,128)S(1)} %get-tuple-element.351), kind=kOutput, calls=%fused_computation.36 | convolution fusion | flops 12885164032 | bytes 17825792 | tf_op jit(solution)/shard_map/fn,bfc->bnc/dot_general | solution.py:162
  282.2 2.4 copy.48
  284.7 37.5 %while.30 = (s32[]{:T(128)}, f32[512,256]{1,0:T(8,128)S(1)}, s32[]{:T(128)}, bf16[16,512,256]{2,1,0:T(8,128)(2,1)}, bf16[8192,256]{1,0:T(8,128)(2,1)}, /*index=5...) while((s32[]{:T(128)}, f32[512,256]{1,0:T(8,128)S(1)}, s32[]{:T(128)}, ...), condition=%wide.region_1.2_spmd.clone, body=%wide.region_0.1_spmd.clone.sunk | while | flops 1310987 | bytes 4719323 | solution.py:116
  284.7 1.1 dynamic-slice_convert_fusion.9
  287.1 1.0 dynamic-slice_convert_fusion.9
  289.5 1.0 dynamic-slice_convert_fusion.9
  291.8 1.0 dynamic-slice_convert_fusion.9
  294.1 1.0 dynamic-slice_convert_fusion.9
  296.5 1.0 dynamic-slice_convert_fusion.9
  298.8 1.0 dynamic-slice_convert_fusion.9
  301.1 1.0 dynamic-slice_convert_fusion.9
  303.5 1.0 dynamic-slice_convert_fusion.9
  305.8 1.0 dynamic-slice_convert_fusion.9
  308.1 1.0 dynamic-slice_convert_fusion.9
  310.5 1.0 dynamic-slice_convert_fusion.9
  312.8 1.0 dynamic-slice_convert_fusion.9
  315.2 1.0 dynamic-slice_convert_fusion.9
  317.5 1.0 dynamic-slice_convert_fusion.9
  319.8 1.0 dynamic-slice_convert_fusion.9
  320.8 1.0 dynamic-slice_convert_fusion.8
  323.6 1.3 collective-permute-start.1
  325.1 20.4 %collective-permute-done.1 = bf16[2,768]{0,1:T(8,128)(2,1)S(1)} collective-permute-done((bf16[2,768]{0,1:T(8,128)(2,1)S(1)}, bf16[2,768]{0,1:T(8,128)(2,1)S(1)}, u32[]{:S(2)}, u32[]{:S(2)}) %collective-permute-start.1) | collective-permute-done | bytes 3104 | tf_op jit(solution)/shard_map/ppermute | solution.py:11
  347.8 40.5 %reduce-scatter.2.cloned.1.call-done = bf16[256,256]{1,0:T(8,128)(2,1)} async-done(((bf16[4096,256]{1,0:T(8,128)(2,1)}), bf16[256,256]{1,0:T(8,128)(2,1)}) %reduce-scatter.2.cloned.1.call-update) | async-done | bytes 131088 | tf_op jit(solution)/shard_map/reduce_scatter | solution.py:166
  388.3 1.6 convert_element_type.164
  (217 shorter events, 61.8 us)
Async XLA Ops:
  7.2 56.6 %all-gather.3.cloned.1.call-start = ((), (), s32[]{:S(2)}) async-start(), calls=%async_computation.2 | async-start | bytes 2228224 | tf_op jit(solution)/shard_map/all_gather | solution.py:79
  7.9 8.8 %copy-start.8 = (f32[3,3,256]{2,1,0:T(4,128)S(1)}, f32[3,3,256]{2,1,0:T(4,128)}, u32[]{:S(2)}) copy-start(f32[3,3,256]{2,1,0:T(4,128)} %param.11) | copy-start | bytes 27652
  18.8 57.5 %copy-start.5 = (bf16[256,256]{1,0:T(8,128)(2,1)}, bf16[256,256]{1,0:T(8,128)(2,1)S(1)}, u32[]{:S(2)}) copy-start(bf16[256,256]{1,0:T(8,128)(2,1)S(1)} %select_convert_fusion) | copy-start | bytes 393220
  69.0 5.3 %collective-permute-start = (bf16[2,768]{1,0:T(2,128)(2,1)S(1)}, bf16[2,768]{1,0:T(2,128)(2,1)S(1)}, u32[]{:S(2)}, u32[]{:S(2)}) collective-permute-start(bf16[2,768]{1,0:T(2,128)(2,1)S(1)} %slice.215), channel_id=1, source_target_pairs={{0,16},{16,32},{32,48},{48,64},{64,80},{80,96},{96,112},{112,128},... | collective-permute-start | bytes 9224 | tf_op jit(solution)/shard_map/ppermute | solution.py:11
  76.4 3.7 copy-start.1
  80.1 9.9 %slice-start = ((bf16[4096,256]{1,0:T(8,128)(2,1)}), bf16[3840,256]{1,0:T(8,128)(2,1)S(1)}, s32[]{:S(2)}) async-start(bf16[4096,256]{1,0:T(8,128)(2,1)} %param.12), calls=%async_computation.5 | async-start | bytes 3932160 | tf_op jit(solution)/shard_map/slice | solution.py:100
  80.1 110.1 %all-to-all-start = ((bf16[16,512,256]{2,1,0:T(8,128)(2,1)}), bf16[16,512,256]{2,1,0:T(8,128)(2,1)}, u32[]{:S(2)}, u32[]{:S(2)}) async-start(bf16[16,512,256]{2,1,0:T(8,128)(2,1)} %stack.11), calls=%async_computation | async-start | bytes 8388608 | tf_op jit(solution)/shard_map/all_to_all | solution.py:139
  89.7 194.9 %all-gather.5.cloned.1.call-start = ((), (), s32[]{:S(2)}) async-start(), calls=%async_computation.3 | async-start | bytes 4456448 | tf_op jit(solution)/shard_map/all_gather | solution.py:106
  98.4 13.2 %copy-start.3 = (bf16[512,512]{1,0:T(8,128)(2,1)}, bf16[512,512]{1,0:T(8,128)(2,1)S(1)}, u32[]{:S(2)}) copy-start(bf16[512,512]{1,0:T(8,128)(2,1)S(1)} %fusion.20) | copy-start | bytes 1572868
  113.6 274.7 %reduce-scatter.2.cloned.1.call-start = ((), (), s32[]{:S(2)}) async-start(), calls=%async_computation.4 | async-start | bytes 2228224 | tf_op jit(solution)/shard_map/reduce_scatter | solution.py:166
  190.2 4.1 %copy-start = (bf16[512,256]{1,0:T(8,128)(2,1)S(1)}, bf16[512,256]{1,0:T(8,128)(2,1)}, u32[]{:S(2)}) copy-start(bf16[512,256]{1,0:T(8,128)(2,1)} %convolution_convert_fusion.2) | copy-start | bytes 786436
  284.6 37.5 %copy-start.2 = (f32[256,3,256]{2,0,1:T(8,128)S(1)}, f32[256,3,256]{2,0,1:T(8,128)}, u32[]{:S(2)}) copy-start(f32[256,3,256]{2,0,1:T(8,128)} %copy-done.1) | copy-start | bytes 2359300
  284.6 37.5 %copy-start.4 = (bf16[512,512]{1,0:T(8,128)(2,1)S(1)}, bf16[512,512]{1,0:T(8,128)(2,1)}, u32[]{:S(2)}) copy-start(bf16[512,512]{1,0:T(8,128)(2,1)} %copy-done.3) | copy-start | bytes 1572868
  284.6 37.8 %copy-start.6 = (bf16[256,256]{1,0:T(8,128)(2,1)S(1)}, bf16[256,256]{1,0:T(8,128)(2,1)}, u32[]{:S(2)}) copy-start(bf16[256,256]{1,0:T(8,128)(2,1)} %copy-done.5) | copy-start | bytes 393220
  284.6 38.7 %copy-start.7 = (bf16[256,256]{1,0:T(8,128)(2,1)S(1)}, bf16[256,256]{1,0:T(8,128)(2,1)}, u32[]{:S(2)}) copy-start(bf16[256,256]{1,0:T(8,128)(2,1)} %param.13) | copy-start | bytes 393220
  323.6 21.8 %collective-permute-start.1 = (bf16[2,768]{0,1:T(8,128)(2,1)S(1)}, bf16[2,768]{0,1:T(8,128)(2,1)S(1)}, u32[]{:S(2)}, u32[]{:S(2)}) collective-permute-start(bf16[2,768]{0,1:T(8,128)(2,1)S(1)} %copy.43), channel_id=1, source_target_pairs={{16,0},{32,16},{48,32},{64,48},{80,64},{96,80},{112,96},{128,112},... | collective-permute-start | bytes 9224 | tf_op jit(solution)/shard_map/ppermute | solution.py:11
Sparse Core Ops, SparseCore 0:
  10.5 53.1 all-gather.2
  113.7 149.1 all-gather.4
  284.7 103.5 reduce-scatter.1
